TPU v7x, 512 devices: a whole 4x4x16 slice. The times are simulated.
512 devices in a mesh: line: 32 (over z, core), scan: 16 (over x, y).
Axes of the slice: x: 4, y: 4, z: 16, core: 2. Of those that a mesh axis runs over, the one named last changes fastest.
Arguments:
- query_row: bfloat16 [32, 2048, 512], P('line', 'scan'), may hold values from -6 to 6
- key_row: bfloat16 [32, 2048, 512], P('line', 'scan'), may hold values from -6 to 6
- value_row: bfloat16 [32, 2048, 512], P('line', 'scan'), may hold values from -6 to 6
- decay_row: float32 [32, 2048, 4], P('line', 'scan'), may hold values from -2 to 0
- beta_row: float32 [32, 2048, 4], P('line', 'scan'), may hold values from 0.02 to 0.2
- gain_row: float32 [128], replicated, may hold values from 0.1 to 1.9
- query_col: bfloat16 [32, 16, 128, 512], P(None, 'scan', 'line'), may hold values from -6 to 6
- key_col: bfloat16 [32, 16, 128, 512], P(None, 'scan', 'line'), may hold values from -6 to 6
- decay_col: float32 [32, 16, 128, 4], P(None, 'scan', 'line'), may hold values from -2 to 0
- beta_col: float32 [32, 16, 128, 4], P(None, 'scan', 'line'), may hold values from 0.02 to 0.2
- gain_col: float32 [128], replicated, may hold values from 0.1 to 1.9
Outputs:
- mixed: bfloat16 [32, 2048, 512], P('line', 'scan')
All inputs are finite; a program needn't handle non-finite values.
Results may differ from a plain program's by a relative error of at most 0.0049.
Values may be sent and summed in bfloat16 or wider, within the bound.
No kernel may reach another device: no remote copies, remote signals or barrier semaphores. Data moves between devices by JAX's collectives and lax.ppermute only.
A program may use at most 64 MiB of HBM per device.

v0:
```python
import jax
import jax.numpy as jnp
from jax import lax
from jax.sharding import PartitionSpec as P

HIGHEST = lax.Precision.HIGHEST
BASE_BLOCK = 16


def from_behind(block, axis, distance):
    devices = range(lax.axis_size(axis))
    route = [(i - distance, i) for i in devices if i - distance in devices]
    return lax.ppermute(block, axis, route)


def matmul(spec, left, right):
    return jnp.einsum(spec, left, right, precision=HIGHEST)


def unit_lower_inverse(system):
    batch = system.shape[:-2]
    size = system.shape[-1]
    base = min(BASE_BLOCK, size)
    count = size // base
    assert count * base == size and count & count - 1 == 0
    eye = jnp.eye(base, dtype=jnp.float32)
    grid = system.reshape(batch + (count, base, count, base))
    diagonal = jnp.moveaxis(jnp.diagonal(grid, axis1=-4, axis2=-2), -1, -3)
    lower = diagonal - eye
    inverse = eye - lower
    power = lower
    reach = 2
    while reach < base:
        power = matmul("...ij,...jk->...ik", power, power)
        inverse = inverse + matmul("...ij,...jk->...ik", inverse, power)
        reach *= 2
    width = base
    while width < size:
        pairs = size // (2 * width)
        grid = system.reshape(batch + (pairs, 2, width, pairs, 2, width))
        coupling = jnp.moveaxis(jnp.diagonal(grid, axis1=-6, axis2=-3), -1, -5)[..., 1, :, 0, :]
        halves = inverse.reshape(batch + (pairs, 2, width, width))
        upper_inverse = halves[..., 0, :, :]
        lower_inverse = halves[..., 1, :, :]
        mixed = -matmul(
            "...ij,...jk->...ik",
            matmul("...ij,...jk->...ik", lower_inverse, coupling),
            upper_inverse,
        )
        top = jnp.concatenate([upper_inverse, jnp.zeros_like(upper_inverse)], axis=-1)
        bottom = jnp.concatenate([mixed, lower_inverse], axis=-1)
        inverse = jnp.concatenate([top, bottom], axis=-2)
        width *= 2
    return inverse.reshape(batch + (size, size))


def block_system(key_block, log_decay, beta_block):
    key_unit = key_block / jnp.sqrt(jnp.sum(key_block * key_block, axis=-1, keepdims=True) + 1e-06)
    cumulative = jnp.cumsum(log_decay, axis=-1)
    sequence_length = key_block.shape[1]
    lower_mask = jnp.tril(jnp.ones((sequence_length, sequence_length), dtype=jnp.bool_))
    strict = jnp.tril(jnp.ones((sequence_length, sequence_length), dtype=jnp.bool_), -1)
    spread = cumulative[:, :, None] - cumulative[:, None, :]
    ratios = jnp.where(lower_mask, jnp.exp(jnp.where(lower_mask, spread, 0.0)), 0.0)
    key_inner = matmul("bik,bjk->bij", key_unit, key_unit)
    system = jnp.where(strict, beta_block[:, :, None] * ratios * key_inner, 0.0) + jnp.eye(
        sequence_length, dtype=jnp.float32
    )
    return (key_unit, cumulative, ratios, unit_lower_inverse(system))


def block_terms(query_block, key_block, value_block, log_decay, beta_block):
    key_unit, cumulative, ratios, system_inverse = block_system(key_block, log_decay, beta_block)
    growth = jnp.exp(cumulative)
    right_side = jnp.concatenate(
        [beta_block[:, :, None] * value_block, (beta_block * growth)[:, :, None] * key_unit],
        axis=-1,
    )
    solved = matmul("bij,bjv->biv", system_inverse, right_side)
    value_size = value_block.shape[-1]
    updates = solved[:, :, :value_size]
    weighted = solved[:, :, value_size:]
    attend = ratios * matmul("bik,bjk->bij", query_block, key_unit)
    local_out = matmul("bij,bjv->biv", attend, updates)
    state_query = growth[:, :, None] * query_block - matmul("bij,bjk->bik", attend, weighted)
    key_tail = jnp.exp(cumulative[:, -1:] - cumulative)[:, :, None] * key_unit
    return (local_out, state_query, key_tail, weighted, updates, growth[:, -1])


def column_operator(query_block, key_block, log_decay, beta_block):
    key_unit, cumulative, ratios, system_inverse = block_system(key_block, log_decay, beta_block)
    attend = ratios * matmul("bik,bjk->bij", query_block, key_unit)
    return matmul("bij,bjk->bik", attend, system_inverse) * beta_block[:, None, :]


def to_heads(array, leading_count, sequence_length, head_count, head_size):
    shaped = array.astype(jnp.float32).reshape(
        leading_count, sequence_length, head_count, head_size
    )
    return shaped.transpose(0, 2, 1, 3).reshape(
        leading_count * head_count, sequence_length, head_size
    )


def gates_to_heads(array, leading_count, sequence_length, head_count):
    return array.transpose(0, 2, 1).reshape(leading_count * head_count, sequence_length)


def from_heads(array, leading_count, sequence_length, head_count, head_size):
    return array.reshape(leading_count, head_count, sequence_length, head_size).transpose(
        0, 2, 1, 3
    )


def head_norm(array, gain):
    return array * lax.rsqrt(jnp.mean(array * array, axis=-1, keepdims=True) + 1e-05) * gain


def prefix_states(transfer, offset):
    scan_count = lax.axis_size("scan")
    head_size = offset.shape[-1]
    distance = 1
    while distance < scan_count:
        if 2 * distance < scan_count:
            arrived = from_behind(jnp.concatenate([transfer, offset], axis=-1), "scan", distance)
            composed = matmul("bij,bjv->biv", transfer, arrived)
            transfer = composed[:, :, :head_size]
            offset = composed[:, :, head_size:] + offset
        else:
            arrived = from_behind(offset, "scan", distance)
            offset = matmul("bij,bjv->biv", transfer, arrived) + offset
        distance *= 2
    return from_behind(offset, "scan", 1)


def shards(
    query_row,
    key_row,
    value_row,
    decay_row,
    beta_row,
    gain_row,
    query_col,
    key_col,
    decay_col,
    beta_col,
    gain_col,
):
    row_count, segment, features = query_row.shape
    head_size = gain_row.shape[0]
    head_count = features // head_size
    line_count = lax.axis_size("line")
    total_rows = query_col.shape[0]
    column_count = query_col.shape[2]

    def columns(array):
        return array.reshape(total_rows, column_count, -1).transpose(1, 0, 2)

    local_out, state_query, key_tail, weighted, updates, ending = block_terms(
        to_heads(query_row, row_count, segment, head_count, head_size),
        to_heads(key_row, row_count, segment, head_count, head_size),
        to_heads(value_row, row_count, segment, head_count, head_size),
        gates_to_heads(decay_row, row_count, segment, head_count),
        gates_to_heads(beta_row, row_count, segment, head_count),
    )
    identity = jnp.broadcast_to(
        jnp.eye(head_size, dtype=jnp.float32), (row_count * head_count, head_size, head_size)
    )
    transfer = ending[:, None, None] * identity - matmul("bjk,bjl->bkl", key_tail, weighted)
    offset = matmul("bjk,bjv->bkv", key_tail, updates)
    operator = column_operator(
        to_heads(columns(query_col), column_count, total_rows, head_count, head_size),
        to_heads(columns(key_col), column_count, total_rows, head_count, head_size),
        gates_to_heads(columns(decay_col), column_count, total_rows, head_count),
        gates_to_heads(columns(beta_col), column_count, total_rows, head_count),
    )
    incoming = prefix_states(transfer, offset)
    row_out = local_out + matmul("bik,bkv->biv", state_query, incoming)
    row_scan = from_heads(row_out, row_count, segment, head_count, head_size)
    values_col = (
        head_norm(row_scan, gain_row).reshape(row_count, segment, features).astype(jnp.bfloat16)
    )
    arranged = values_col.reshape(row_count, line_count, segment // line_count, features)
    column_values = lax.all_to_all(arranged, "line", split_axis=1, concat_axis=0, tiled=True)
    col_out = matmul(
        "bij,bjv->biv",
        operator,
        to_heads(columns(column_values), column_count, total_rows, head_count, head_size),
    )
    col_scan = from_heads(col_out, column_count, total_rows, head_count, head_size)
    normed = (
        head_norm(col_scan, gain_col)
        .transpose(1, 0, 2, 3)
        .reshape(total_rows, 1, column_count, features)
        .astype(jnp.bfloat16)
    )
    returned = lax.all_to_all(normed, "line", split_axis=0, concat_axis=1, tiled=True)
    return returned.reshape(row_count, segment, features)


def solution(mesh):
    placed = (
        P("line", "scan", None),
        P("line", "scan", None),
        P("line", "scan", None),
        P("line", "scan", None),
        P("line", "scan", None),
        P(),
        P(None, "scan", "line", None),
        P(None, "scan", "line", None),
        P(None, "scan", "line", None),
        P(None, "scan", "line", None),
        P(),
    )
    return jax.shard_map(
        shards, mesh=mesh, in_specs=placed, out_specs=P("line", "scan", None), check_vma=False
    )
```

profile of v0, /device:TPU:6, one launch (start us, length us, event | category | flops | bytes accessed | tf_op | source)
XLA Modules:
  0.0 160.5 jit_solution(16315347786779798503)
XLA Ops:
  0.0 0.8 fusion.86
  1.2 1.0 reduce_window_sum.23
  2.1 1.5 fusion.5
  4.2 1.7 %copy.195 = f32[4,8,16,8,16]{4,2,3,1,0:T(8,128)} copy(f32[4,8,16,8,16]{4,3,2,1,0:T(8,128)S(1)} %reshape.334) | data formatting | bytes 524288 | tf_op jit(solution)/shard_map/reshape | solution.py:27
  5.9 2.2 %gather_fusion.1 = f32[8,4,16,16]{3,2,1,0:T(8,128)S(1)} fusion(f32[4,16,16,8,8]{2,1,4,3,0:T(8,128)} %bitcast.193, s32[8]{0:T(128)S(1)} %or_bitcast_fusion.1), kind=kCustom, calls=%fused_computation.1 | custom fusion | bytes 65600 | tf_op jit(solution)/shard_map/jit(diagonal)/gather | solution.py:28
  9.3 2.7 %reshape.336 = f32[4,4,2,16,4,2,16]{6,5,4,3,2,1,0:T(2,128)S(1)} reshape(f32[4,128,128]{2,1,0:T(8,128)S(1)} %fusion.5) | data formatting | bytes 524288 | tf_op jit(solution)/shard_map/reshape | solution.py:40
  12.0 1.8 %reshape.338 = f32[4,2,2,32,2,2,32]{6,5,4,3,2,1,0:T(2,128)} reshape(f32[4,128,128]{2,1,0:T(8,128)S(1)} %fusion.5) | data formatting | bytes 524288 | tf_op jit(solution)/shard_map/reshape | solution.py:40
  13.8 1.1 transpose.144
  16.3 1.7 %copy.194 = f32[4,4,2,16,4,2,16]{6,3,4,1,5,2,0:T(8,128)} copy(f32[4,4,2,16,4,2,16]{6,5,4,3,2,1,0:T(2,128)S(1)} %reshape.336) | data formatting | bytes 524288 | tf_op jit(solution)/shard_map/reshape | solution.py:40
  18.0 2.2 %gather_fusion.2 = f32[4,4,2,16,2,16]{5,3,4,2,1,0:T(8,128)S(1)} fusion(f32[4,2,16,2,16,4,4]{4,2,6,5,3,1,0:T(8,128)} %bitcast.192, s32[4]{0:T(128)S(1)} %or_bitcast_fusion), kind=kCustom, calls=%fused_computation.2 | custom fusion | bytes 131104 | tf_op jit(solution)/shard_map/jit(diagonal)/gather | solution.py:41
  22.9 1.0 slice.234
  25.7 0.8 fusion.32
  26.8 0.7 convolution_subtract_fusion
  27.5 0.8 pad_maximum_fusion
  28.4 3.7 %collective-permute-start = (f32[4,128,256]{2,1,0:T(8,128)}, f32[4,128,256]{2,1,0:T(8,128)}, u32[]{:S(2)}, u32[]{:S(2)}) collective-permute-start(f32[4,128,256]{2,1,0:T(8,128)} %pad_maximum_fusion), channel_id=1, source_target_pairs={{0,1},{1,2},{2,3},{3,4},{4,5},{5,6},{6,7},{7,8},{8,9},{9,10},{10,1... | collective-permute-start | bytes 1572872 | tf_op jit(solution)/shard_map/ppermute | solution.py:13
  37.7 8.6 %collective-permute-done = f32[4,128,256]{2,1,0:T(8,128)} collective-permute-done((f32[4,128,256]{2,1,0:T(8,128)}, f32[4,128,256]{2,1,0:T(8,128)}, u32[]{:S(2)}, u32[]{:S(2)}) %collective-permute-start) | collective-permute-done | bytes 524320 | tf_op jit(solution)/shard_map/ppermute | solution.py:13
  46.3 2.1 %fusion.93 = f32[4,128,256]{1,2,0:T(8,128)S(1)} fusion(f32[4,128,128]{2,1,0:T(8,128)S(1)} %convolution_subtract_fusion, f32[4,128,256]{2,1,0:T(8,128)} %collective-permute-done), kind=kOutput, calls=%fused_computation.184 | convolution fusion | flops 201326592 | bytes 1310720 | tf_op jit(solution)/shard_map/bij,bjv->biv/dot_general | solution.py:17
  48.5 3.0 %collective-permute-start.1 = (f32[4,128,256]{1,2,0:T(8,128)S(1)}, f32[4,128,256]{1,2,0:T(8,128)S(1)}, u32[]{:S(2)}, u32[]{:S(2)}) collective-permute-start(f32[4,128,256]{1,2,0:T(8,128)S(1)} %pad_maximum_fusion.1), channel_id=1, source_target_pairs={{0,2},{1,3},{2,4},{3,5},{4,6},{5,7},{6,8},{7,9},{8,10},{9,11},{10,... | collective-permute-start | bytes 1572872 | tf_op jit(solution)/shard_map/ppermute | solution.py:13
  52.6 13.0 %collective-permute-done.1 = f32[4,128,256]{1,2,0:T(8,128)S(1)} collective-permute-done((f32[4,128,256]{1,2,0:T(8,128)S(1)}, f32[4,128,256]{1,2,0:T(8,128)S(1)}, u32[]{:S(2)}, u32[]{:S(2)}) %collective-permute-start.1) | collective-permute-done | bytes 524320 | tf_op jit(solution)/shard_map/ppermute | solution.py:13
  66.3 0.8 pad_maximum_fusion.2
  67.1 1.3 collective-permute-start.2
  69.6 11.5 %collective-permute-done.2 = f32[4,128,256]{1,2,0:T(8,128)} collective-permute-done((f32[4,128,256]{1,2,0:T(8,128)}, f32[4,128,256]{1,2,0:T(8,128)}, u32[]{:S(2)}, u32[]{:S(2)}) %collective-permute-start.2) | collective-permute-done | bytes 524320 | tf_op jit(solution)/shard_map/ppermute | solution.py:13
  81.2 1.7 %fusion.75 = f32[4,128,256]{2,1,0:T(8,128)S(1)} fusion(f32[4,128,256]{1,2,0:T(8,128)} %collective-permute-done.2, f32[4,128,256]{1,2,0:T(8,128)S(1)} %fusion.77), kind=kOutput, calls=%fused_computation.166 | convolution fusion | flops 201326592 | bytes 1310720 | tf_op jit(solution)/shard_map/bij,bjv->biv/dot_general | solution.py:17
  83.0 1.3 collective-permute-start.3
  85.2 7.6 %collective-permute-done.3 = f32[4,128,128]{1,2,0:T(8,128)S(1)} collective-permute-done((f32[4,128,128]{1,2,0:T(8,128)S(1)}, f32[4,128,128]{1,2,0:T(8,128)S(1)}, u32[]{:S(2)}, u32[]{:S(2)}) %collective-permute-start.3) | collective-permute-done | bytes 262176 | tf_op jit(solution)/shard_map/ppermute | solution.py:13
  93.6 2.1 %collective-permute-start.4 = (f32[4,128,128]{1,2,0:T(8,128)S(1)}, f32[4,128,128]{1,2,0:T(8,128)S(1)}, u32[]{:S(2)}, u32[]{:S(2)}) collective-permute-start(f32[4,128,128]{1,2,0:T(8,128)S(1)} %convolution_add_fusion.7), channel_id=1, source_target_pairs={{0,1},{1,2},{2,3},{3,4},{4,5},{5,6},{6,7},{7,8},{8,9},{9,10},{10,1... | collective-permute-start | bytes 786440 | tf_op jit(solution)/shard_map/ppermute | solution.py:13
  96.1 8.0 %collective-permute-done.4 = f32[4,128,128]{1,2,0:T(8,128)S(1)} collective-permute-done((f32[4,128,128]{1,2,0:T(8,128)S(1)}, f32[4,128,128]{1,2,0:T(8,128)S(1)}, u32[]{:S(2)}, u32[]{:S(2)}) %collective-permute-start.4) | collective-permute-done | bytes 262176 | tf_op jit(solution)/shard_map/ppermute | solution.py:13
  105.0 0.7 convert_element_type.90
  105.7 15.5 %all-to-all-start = ((bf16[1,32,4,512]{3,2,0,1:T(4,128)(2,1)}), bf16[1,32,4,512]{3,2,0,1:T(4,128)(2,1)S(1)}, u32[]{:S(2)}, u32[]{:S(2)}) async-start(bf16[1,32,4,512]{3,2,0,1:T(4,128)(2,1)} %bitcast.66), calls=%async_computation | async-start | bytes 262144 | tf_op jit(solution)/shard_map/all_to_all | solution.py:184
  122.2 16.2 %all-to-all-done = bf16[1,32,4,512]{3,2,0,1:T(4,128)(2,1)S(1)} async-done(((bf16[1,32,4,512]{3,2,0,1:T(4,128)(2,1)}), bf16[1,32,4,512]{3,2,0,1:T(4,128)(2,1)S(1)}, u32[]{:S(2)}, u32[]{:S(2)}) %all-to-all-start) | async-done | bytes 131104 | tf_op jit(solution)/shard_map/all_to_all | solution.py:184
  139.6 20.2 %all_to_all.8 = bf16[32,1,4,512]{3,2,1,0:T(4,128)(2,1)S(1)} all-to-all(bf16[32,1,4,512]{3,2,1,0:T(4,128)(2,1)S(1)} %copy.160), channel_id=1, replica_groups=mesh['line'=32,'scan'=16] {'line'}, dimensions={0} | all-to-all | bytes 262144 | tf_op jit(solution)/shard_map/all_to_all | solution.py:197
  159.8 0.7 reshape.350
  (163 shorter events, 21.4 us)
Async XLA Ops:
  1.0 25.8 %copy-start.20 = (f32[4,128]{1,0:T(4,128)}, f32[4,128]{1,0:T(4,128)S(1)}, u32[]{:S(2)}) copy-start(f32[4,128]{1,0:T(4,128)S(1)} %sqrt_bitcast_fusion) | copy-start | bytes 6148
  1.1 4.8 %copy-start.17 = (pred[128,128]{1,0:T(8,128)(4,1)}, pred[128,128]{1,0:T(8,128)(4,1)S(1)}, u32[]{:S(2)}) copy-start(pred[128,128]{1,0:T(8,128)(4,1)S(1)} %get-tuple-element.57) | copy-start | bytes 49156
  22.2 2.4 %copy-start.2 = (bf16[1,128,512]{2,1,0:T(8,128)(2,1)S(1)}, bf16[1,128,512]{2,1,0:T(8,128)(2,1)}, u32[]{:S(2)}) copy-start(bf16[1,128,512]{2,1,0:T(8,128)(2,1)} %param.13) | copy-start | bytes 393220
  22.3 2.3 %copy-start.22 = (f32[1,128,4]{1,2,0:T(4,128)S(1)}, f32[1,128,4]{1,2,0:T(4,128)}, u32[]{:S(2)}) copy-start(f32[1,128,4]{1,2,0:T(4,128)} %param.15) | copy-start | bytes 6148
  25.6 6.4 %copy-start.1 = (bf16[1,128,512]{2,1,0:T(8,128)(2,1)S(1)}, bf16[1,128,512]{2,1,0:T(8,128)(2,1)}, u32[]{:S(2)}) copy-start(bf16[1,128,512]{2,1,0:T(8,128)(2,1)} %param.11) | copy-start | bytes 393220
  25.7 7.1 %copy-start.7 = (bf16[32,1,4,512]{3,2,1,0:T(4,128)(2,1)S(1)}, bf16[32,1,4,512]{3,2,1,0:T(4,128)(2,1)}, u32[]{:S(2)}) copy-start(bf16[32,1,4,512]{3,2,1,0:T(4,128)(2,1)} %param.18) | copy-start | bytes 393220
  26.6 6.5 %copy-start.25 = (f32[32,1,4,4]{0,3,2,1:T(4,128)S(1)}, f32[32,1,4,4]{0,3,2,1:T(4,128)}, u32[]{:S(2)}) copy-start(f32[32,1,4,4]{0,3,2,1:T(4,128)} %param.19) | copy-start | bytes 6148
  26.6 6.7 %copy-start.19 = (f32[32,1,4,4]{0,3,2,1:T(4,128)S(1)}, f32[32,1,4,4]{0,3,2,1:T(4,128)}, u32[]{:S(2)}) copy-start(f32[32,1,4,4]{0,3,2,1:T(4,128)} %param.20) | copy-start | bytes 6148
  28.4 18.0 %collective-permute-start = (f32[4,128,256]{2,1,0:T(8,128)}, f32[4,128,256]{2,1,0:T(8,128)}, u32[]{:S(2)}, u32[]{:S(2)}) collective-permute-start(f32[4,128,256]{2,1,0:T(8,128)} %pad_maximum_fusion), channel_id=1, source_target_pairs={{0,1},{1,2},{2,3},{3,4},{4,5},{5,6},{6,7},{7,8},{8,9},{9,10},{10,1... | collective-permute-start | bytes 1572872 | tf_op jit(solution)/shard_map/ppermute | solution.py:13
  48.5 17.1 %collective-permute-start.1 = (f32[4,128,256]{1,2,0:T(8,128)S(1)}, f32[4,128,256]{1,2,0:T(8,128)S(1)}, u32[]{:S(2)}, u32[]{:S(2)}) collective-permute-start(f32[4,128,256]{1,2,0:T(8,128)S(1)} %pad_maximum_fusion.1), channel_id=1, source_target_pairs={{0,2},{1,3},{2,4},{3,5},{4,6},{5,7},{6,8},{7,9},{8,10},{9,11},{10,... | collective-permute-start | bytes 1572872 | tf_op jit(solution)/shard_map/ppermute | solution.py:13
  52.6 15.8 %copy-start.13 = (bf16[1,128,128]{2,1,0:T(8,128)(2,1)S(1)}, bf16[1,128,128]{2,1,0:T(8,128)(2,1)}, u32[]{:S(2)}) copy-start(bf16[1,128,128]{2,1,0:T(8,128)(2,1)} %get-tuple-element.41) | copy-start | bytes 98308
  52.6 15.8 %copy-start.14 = (bf16[1,128,128]{2,1,0:T(8,128)(2,1)S(1)}, bf16[1,128,128]{2,1,0:T(8,128)(2,1)}, u32[]{:S(2)}) copy-start(bf16[1,128,128]{2,1,0:T(8,128)(2,1)} %get-tuple-element.42) | copy-start | bytes 98308
  52.6 15.8 %copy-start.15 = (bf16[1,128,128]{2,1,0:T(8,128)(2,1)S(1)}, bf16[1,128,128]{2,1,0:T(8,128)(2,1)}, u32[]{:S(2)}) copy-start(bf16[1,128,128]{2,1,0:T(8,128)(2,1)} %get-tuple-element.43) | copy-start | bytes 98308
  52.6 15.8 %copy-start.16 = (bf16[1,128,128]{2,1,0:T(8,128)(2,1)S(1)}, bf16[1,128,128]{2,1,0:T(8,128)(2,1)}, u32[]{:S(2)}) copy-start(bf16[1,128,128]{2,1,0:T(8,128)(2,1)} %get-tuple-element.44) | copy-start | bytes 98308
  66.2 2.9 %copy-start.18 = (pred[128,128]{1,0:T(8,128)(4,1)S(1)}, pred[128,128]{1,0:T(8,128)(4,1)}, u32[]{:S(2)}) copy-start(pred[128,128]{1,0:T(8,128)(4,1)} %copy-done.17) | copy-start | bytes 49156
  66.2 2.9 %copy-start.21 = (f32[4,128]{1,0:T(4,128)S(1)}, f32[4,128]{1,0:T(4,128)}, u32[]{:S(2)}) copy-start(f32[4,128]{1,0:T(4,128)} %copy-done.20) | copy-start | bytes 6148
  67.1 14.1 %collective-permute-start.2 = (f32[4,128,256]{1,2,0:T(8,128)}, f32[4,128,256]{1,2,0:T(8,128)}, u32[]{:S(2)}, u32[]{:S(2)}) collective-permute-start(f32[4,128,256]{1,2,0:T(8,128)} %pad_maximum_fusion.2), channel_id=1, source_target_pairs={{0,4},{1,5},{2,6},{3,7},{4,8},{5,9},{6,10},{7,11},{8,12},{9,13},{1... | collective-permute-start | bytes 1572872 | tf_op jit(solution)/shard_map/ppermute | solution.py:13
  82.8 12.8 %copy-start.5 = (f32[1,128,128]{2,1,0:T(8,128)S(1)}, f32[1,128,128]{2,1,0:T(8,128)}, u32[]{:S(2)}) copy-start(f32[1,128,128]{2,1,0:T(8,128)} %get-tuple-element.31) | copy-start | bytes 196612
  82.8 12.8 %copy-start.6 = (f32[1,128,128]{2,1,0:T(8,128)S(1)}, f32[1,128,128]{2,1,0:T(8,128)}, u32[]{:S(2)}) copy-start(f32[1,128,128]{2,1,0:T(8,128)} %get-tuple-element.32) | copy-start | bytes 196612
  83.0 9.8 %collective-permute-start.3 = (f32[4,128,128]{1,2,0:T(8,128)S(1)}, f32[4,128,128]{1,2,0:T(8,128)S(1)}, u32[]{:S(2)}, u32[]{:S(2)}) collective-permute-start(f32[4,128,128]{1,2,0:T(8,128)S(1)} %add.162), channel_id=1, source_target_pairs={{0,8},{1,9},{2,10},{3,11},{4,12},{5,13},{6,14},{7,15},{16,24},{17,... | collective-permute-start | bytes 786440 | tf_op jit(solution)/shard_map/ppermute | solution.py:13
  84.6 20.2 %copy-start.30 = (f32[128]{0:T(128)S(1)}, f32[128]{0:T(128)}, u32[]{:S(2)}) copy-start(f32[128]{0:T(128)} %param.16) | copy-start | bytes 1540
  93.5 27.8 %copy-start.9 = (bf16[4,32,128]{2,1,0:T(8,128)(2,1)S(1)}, bf16[4,32,128]{2,1,0:T(8,128)(2,1)}, u32[]{:S(2)}) copy-start(bf16[4,32,128]{2,1,0:T(8,128)(2,1)} %get-tuple-element.45) | copy-start | bytes 98308
  93.5 27.8 %copy-start.10 = (bf16[4,32,128]{2,1,0:T(8,128)(2,1)S(1)}, bf16[4,32,128]{2,1,0:T(8,128)(2,1)}, u32[]{:S(2)}) copy-start(bf16[4,32,128]{2,1,0:T(8,128)(2,1)} %get-tuple-element.46) | copy-start | bytes 98308
  93.5 27.8 %copy-start.11 = (bf16[4,32,128]{2,1,0:T(8,128)(2,1)S(1)}, bf16[4,32,128]{2,1,0:T(8,128)(2,1)}, u32[]{:S(2)}) copy-start(bf16[4,32,128]{2,1,0:T(8,128)(2,1)} %get-tuple-element.47) | copy-start | bytes 98308
  93.5 27.8 %copy-start.12 = (bf16[4,32,128]{2,1,0:T(8,128)(2,1)S(1)}, bf16[4,32,128]{2,1,0:T(8,128)(2,1)}, u32[]{:S(2)}) copy-start(bf16[4,32,128]{2,1,0:T(8,128)(2,1)} %get-tuple-element.48) | copy-start | bytes 98308
  93.5 27.8 %copy-start.4 = (f32[4,128,128]{2,1,0:T(8,128)S(1)}, f32[4,128,128]{2,1,0:T(8,128)}, u32[]{:S(2)}) copy-start(f32[4,128,128]{2,1,0:T(8,128)} %copy-done.3) | copy-start | bytes 786436
  93.5 27.8 %copy-start.24 = (f32[16,32]{1,0:T(8,128)S(1)}, f32[16,32]{1,0:T(8,128)}, u32[]{:S(2)}) copy-start(f32[16,32]{1,0:T(8,128)} %copy-done.23) | copy-start | bytes 6148
  93.5 27.8 %copy-start.27 = (f32[16,32]{1,0:T(8,128)S(1)}, f32[16,32]{1,0:T(8,128)}, u32[]{:S(2)}) copy-start(f32[16,32]{1,0:T(8,128)} %copy-done.26) | copy-start | bytes 6148
  93.6 27.8 %copy-start.29 = (pred[32,32]{1,0:T(8,128)(4,1)S(1)}, pred[32,32]{1,0:T(8,128)(4,1)}, u32[]{:S(2)}) copy-start(pred[32,32]{1,0:T(8,128)(4,1)} %copy-done.28) | copy-start | bytes 3076
  93.6 10.5 %collective-permute-start.4 = (f32[4,128,128]{1,2,0:T(8,128)S(1)}, f32[4,128,128]{1,2,0:T(8,128)S(1)}, u32[]{:S(2)}, u32[]{:S(2)}) collective-permute-start(f32[4,128,128]{1,2,0:T(8,128)S(1)} %convolution_add_fusion.7), channel_id=1, source_target_pairs={{0,1},{1,2},{2,3},{3,4},{4,5},{5,6},{6,7},{7,8},{8,9},{9,10},{10,1... | collective-permute-start | bytes 786440 | tf_op jit(solution)/shard_map/ppermute | solution.py:13
  105.7 32.8 %all-to-all-start = ((bf16[1,32,4,512]{3,2,0,1:T(4,128)(2,1)}), bf16[1,32,4,512]{3,2,0,1:T(4,128)(2,1)S(1)}, u32[]{:S(2)}, u32[]{:S(2)}) async-start(bf16[1,32,4,512]{3,2,0,1:T(4,128)(2,1)} %bitcast.66), calls=%async_computation | async-start | bytes 262144 | tf_op jit(solution)/shard_map/all_to_all | solution.py:184
  121.4 17.8 %copy-start.31 = (f32[128]{0:T(128)S(1)}, f32[128]{0:T(128)}, u32[]{:S(2)}) copy-start(f32[128]{0:T(128)} %param.21) | copy-start | bytes 1540
  (6 other events, 9.3 us)
where the time goes:
time: 161 us; the launch traced here: 160 us
  waiting for transfers between devices  65 us (40%)
  starting transfers between devices  26.8 us (17%)
  local copies, waits for them, and re-layouts  23.5 us (15%)
  blocking collectives  20.2 us (13%)
  matrix products  19.1 us (12%)
  other arithmetic  4.77 us (3%)
    ppermute x5, waiting for transfers between devices, from_behind(): return lax.ppermute(block, axis, route)  48.8 us
    all_to_all x1, blocking collectives, shards(): lax.all_to_all(normed, 'line', split_axis=0, concat_axis=1, tiled=True)  20.2 us
    dot_general x36, matrix products, matmul(): return jnp.einsum(spec, left, right, precision=HIGHEST)  19.1 us
    all_to_all x1, waiting for transfers between devices, shards(): lax.all_to_all(arranged, 'line', split_axis=1, concat_axis=0, tiled=True)  16.2 us
    all_to_all x1, starting transfers between devices, shards(): lax.all_to_all(arranged, 'line', split_axis=1, concat_axis=0, tiled=True)  15.5 us
    ppermute x5, starting transfers between devices, from_behind(): return lax.ppermute(block, axis, route)  11.3 us
    reshape x4, local copies, waits for them, and re-layouts, unit_lower_inverse(): grid = system.reshape(batch + (pairs, 2, width, pairs, 2, width))  6.38 us
  transfers between devices with their start and end apart: 6, of which 6 were waited for; matrix products, arithmetic and copies ran while one was open for 6% of the time, Pallas kernels for 0%

commit v1 on v0

--- a/solution.py
+++ b/solution.py
@@ -194,7 +194,10 @@
         .reshape(total_rows, 1, column_count, features)
         .astype(jnp.bfloat16)
     )
-    returned = lax.all_to_all(normed, "line", split_axis=0, concat_axis=1, tiled=True)
+    returned = jnp.concatenate(
+        lax.all_to_all(jnp.stack(jnp.split(normed, lax.axis_size("line"), axis=0)), "line", 0, 0),
+        axis=1,
+    )
     return returned.reshape(row_count, segment, features)
 
 

time: 161 us -> 162 us (level)
    another operation x7 -> x41, local copies, waits for them, and re-layouts: 2.26 us -> 3.32 us
where the time goes in v1:
time: 162 us; the launch traced here: 161 us
  waiting for transfers between devices  64.8 us (40%)
  starting transfers between devices  27 us (17%)
  local copies, waits for them, and re-layouts  24.2 us (15%)
  blocking collectives  20.2 us (12%)
  matrix products  19.1 us (12%)
  other arithmetic  4.79 us (3%)
    ppermute x5, waiting for transfers between devices, from_behind(): return lax.ppermute(block, axis, route)  48.8 us
    all_to_all x1, blocking collectives, shards(): lax.all_to_all(jnp.stack(jnp.split(normed, lax.axis_size('line'), axis=0)...  20.2 us
    dot_general x36, matrix products, matmul(): return jnp.einsum(spec, left, right, precision=HIGHEST)  19.1 us
    all_to_all x1, waiting for transfers between devices, shards(): lax.all_to_all(arranged, 'line', split_axis=1, concat_axis=0, tiled=True)  16 us
    all_to_all x1, starting transfers between devices, shards(): lax.all_to_all(arranged, 'line', split_axis=1, concat_axis=0, tiled=True)  15.7 us
    ppermute x5, starting transfers between devices, from_behind(): return lax.ppermute(block, axis, route)  11.3 us
    reshape x4, local copies, waits for them, and re-layouts, unit_lower_inverse(): grid = system.reshape(batch + (pairs, 2, width, pairs, 2, width))  6.39 us
  transfers between devices with their start and end apart: 6, of which 6 were waited for; matrix products, arithmetic and copies ran while one was open for 6% of the time, Pallas kernels for 0%

profile of v1, /device:TPU:6, one launch (start us, length us, event | category | flops | bytes accessed | tf_op | source)
XLA Modules:
  0.0 161.3 jit_solution(4736426757627806194)
XLA Ops:
  0.0 0.8 fusion.88
  1.2 1.0 reduce_window_sum.23
  2.1 1.5 fusion.5
  4.2 1.7 %copy.192 = f32[4,8,16,8,16]{4,2,3,1,0:T(8,128)} copy(f32[4,8,16,8,16]{4,3,2,1,0:T(8,128)S(1)} %reshape.391) | data formatting | bytes 524288 | tf_op jit(solution)/shard_map/reshape | solution.py:27
  5.9 2.2 %gather_fusion.1 = f32[8,4,16,16]{3,2,1,0:T(8,128)S(1)} fusion(f32[4,16,16,8,8]{2,1,4,3,0:T(8,128)} %bitcast.191, s32[8]{0:T(128)S(1)} %or_bitcast_fusion.1), kind=kCustom, calls=%fused_computation.1 | custom fusion | bytes 65600 | tf_op jit(solution)/shard_map/jit(diagonal)/gather | solution.py:28
  9.3 2.7 %reshape.393 = f32[4,4,2,16,4,2,16]{6,5,4,3,2,1,0:T(2,128)S(1)} reshape(f32[4,128,128]{2,1,0:T(8,128)S(1)} %fusion.5) | data formatting | bytes 524288 | tf_op jit(solution)/shard_map/reshape | solution.py:40
  12.0 1.8 %reshape.395 = f32[4,2,2,32,2,2,32]{6,5,4,3,2,1,0:T(2,128)} reshape(f32[4,128,128]{2,1,0:T(8,128)S(1)} %fusion.5) | data formatting | bytes 524288 | tf_op jit(solution)/shard_map/reshape | solution.py:40
  13.8 1.1 transpose.144
  16.3 1.7 %copy.191 = f32[4,4,2,16,4,2,16]{6,3,4,1,5,2,0:T(8,128)} copy(f32[4,4,2,16,4,2,16]{6,5,4,3,2,1,0:T(2,128)S(1)} %reshape.393) | data formatting | bytes 524288 | tf_op jit(solution)/shard_map/reshape | solution.py:40
  18.0 2.2 %gather_fusion.2 = f32[4,4,2,16,2,16]{5,3,4,2,1,0:T(8,128)S(1)} fusion(f32[4,2,16,2,16,4,4]{4,2,6,5,3,1,0:T(8,128)} %bitcast.190, s32[4]{0:T(128)S(1)} %or_bitcast_fusion), kind=kCustom, calls=%fused_computation.2 | custom fusion | bytes 131104 | tf_op jit(solution)/shard_map/jit(diagonal)/gather | solution.py:41
  22.9 1.0 slice.266
  25.7 0.8 fusion.32
  26.8 0.7 convolution_subtract_fusion
  27.6 0.8 pad_maximum_fusion
  28.4 3.7 %collective-permute-start = (f32[4,128,256]{2,1,0:T(8,128)}, f32[4,128,256]{2,1,0:T(8,128)}, u32[]{:S(2)}, u32[]{:S(2)}) collective-permute-start(f32[4,128,256]{2,1,0:T(8,128)} %pad_maximum_fusion), channel_id=1, source_target_pairs={{0,1},{1,2},{2,3},{3,4},{4,5},{5,6},{6,7},{7,8},{8,9},{9,10},{10,1... | collective-permute-start | bytes 1572872 | tf_op jit(solution)/shard_map/ppermute | solution.py:13
  37.7 8.7 %collective-permute-done = f32[4,128,256]{2,1,0:T(8,128)} collective-permute-done((f32[4,128,256]{2,1,0:T(8,128)}, f32[4,128,256]{2,1,0:T(8,128)}, u32[]{:S(2)}, u32[]{:S(2)}) %collective-permute-start) | collective-permute-done | bytes 524320 | tf_op jit(solution)/shard_map/ppermute | solution.py:13
  46.4 2.1 %fusion.95 = f32[4,128,256]{1,2,0:T(8,128)S(1)} fusion(f32[4,128,128]{2,1,0:T(8,128)S(1)} %convolution_subtract_fusion, f32[4,128,256]{2,1,0:T(8,128)} %collective-permute-done), kind=kOutput, calls=%fused_computation.218 | convolution fusion | flops 201326592 | bytes 1310720 | tf_op jit(solution)/shard_map/bij,bjv->biv/dot_general | solution.py:17
  48.6 3.0 %collective-permute-start.1 = (f32[4,128,256]{1,2,0:T(8,128)S(1)}, f32[4,128,256]{1,2,0:T(8,128)S(1)}, u32[]{:S(2)}, u32[]{:S(2)}) collective-permute-start(f32[4,128,256]{1,2,0:T(8,128)S(1)} %pad_maximum_fusion.1), channel_id=1, source_target_pairs={{0,2},{1,3},{2,4},{3,5},{4,6},{5,7},{6,8},{7,9},{8,10},{9,11},{10,... | collective-permute-start | bytes 1572872 | tf_op jit(solution)/shard_map/ppermute | solution.py:13
  52.7 13.0 %collective-permute-done.1 = f32[4,128,256]{1,2,0:T(8,128)S(1)} collective-permute-done((f32[4,128,256]{1,2,0:T(8,128)S(1)}, f32[4,128,256]{1,2,0:T(8,128)S(1)}, u32[]{:S(2)}, u32[]{:S(2)}) %collective-permute-start.1) | collective-permute-done | bytes 524320 | tf_op jit(solution)/shard_map/ppermute | solution.py:13
  66.3 0.8 pad_maximum_fusion.2
  67.1 1.3 collective-permute-start.2
  69.7 11.5 %collective-permute-done.2 = f32[4,128,256]{1,2,0:T(8,128)} collective-permute-done((f32[4,128,256]{1,2,0:T(8,128)}, f32[4,128,256]{1,2,0:T(8,128)}, u32[]{:S(2)}, u32[]{:S(2)}) %collective-permute-start.2) | collective-permute-done | bytes 524320 | tf_op jit(solution)/shard_map/ppermute | solution.py:13
  81.2 1.7 %fusion.75 = f32[4,128,256]{2,1,0:T(8,128)S(1)} fusion(f32[4,128,256]{1,2,0:T(8,128)} %collective-permute-done.2, f32[4,128,256]{1,2,0:T(8,128)S(1)} %fusion.77), kind=kOutput, calls=%fused_computation.198 | convolution fusion | flops 201326592 | bytes 1310720 | tf_op jit(solution)/shard_map/bij,bjv->biv/dot_general | solution.py:17
  83.1 1.3 collective-permute-start.3
  85.3 7.6 %collective-permute-done.3 = f32[4,128,128]{1,2,0:T(8,128)S(1)} collective-permute-done((f32[4,128,128]{1,2,0:T(8,128)S(1)}, f32[4,128,128]{1,2,0:T(8,128)S(1)}, u32[]{:S(2)}, u32[]{:S(2)}) %collective-permute-start.3) | collective-permute-done | bytes 262176 | tf_op jit(solution)/shard_map/ppermute | solution.py:13
  93.6 2.1 %collective-permute-start.4 = (f32[4,128,128]{1,2,0:T(8,128)S(1)}, f32[4,128,128]{1,2,0:T(8,128)S(1)}, u32[]{:S(2)}, u32[]{:S(2)}) collective-permute-start(f32[4,128,128]{1,2,0:T(8,128)S(1)} %convolution_add_fusion.7), channel_id=1, source_target_pairs={{0,1},{1,2},{2,3},{3,4},{4,5},{5,6},{6,7},{7,8},{8,9},{9,10},{10,1... | collective-permute-start | bytes 786440 | tf_op jit(solution)/shard_map/ppermute | solution.py:13
  96.1 8.0 %collective-permute-done.4 = f32[4,128,128]{1,2,0:T(8,128)S(1)} collective-permute-done((f32[4,128,128]{1,2,0:T(8,128)S(1)}, f32[4,128,128]{1,2,0:T(8,128)S(1)}, u32[]{:S(2)}, u32[]{:S(2)}) %collective-permute-start.4) | collective-permute-done | bytes 262176 | tf_op jit(solution)/shard_map/ppermute | solution.py:13
  105.1 0.7 convert_element_type.88
  105.8 15.7 %all-to-all-start = ((bf16[1,32,4,512]{3,2,0,1:T(4,128)(2,1)}), bf16[1,32,4,512]{3,2,0,1:T(4,128)(2,1)S(1)}, u32[]{:S(2)}, u32[]{:S(2)}) async-start(bf16[1,32,4,512]{3,2,0,1:T(4,128)(2,1)} %bitcast.66), calls=%async_computation | async-start | bytes 262144 | tf_op jit(solution)/shard_map/all_to_all | solution.py:184
  122.5 16.0 %all-to-all-done = bf16[1,32,4,512]{3,2,0,1:T(4,128)(2,1)S(1)} async-done(((bf16[1,32,4,512]{3,2,0,1:T(4,128)(2,1)}), bf16[1,32,4,512]{3,2,0,1:T(4,128)(2,1)S(1)}, u32[]{:S(2)}, u32[]{:S(2)}) %all-to-all-start) | async-done | bytes 131104 | tf_op jit(solution)/shard_map/all_to_all | solution.py:184
  140.5 20.2 %all_to_all.14 = bf16[32,1,1,4,512]{4,3,2,1,0:T(4,128)(2,1)S(1)} all-to-all(bf16[32,1,1,4,512]{4,3,2,1,0:T(4,128)(2,1)S(1)} %constant_dynamic-update-slice_fusion), channel_id=1, replica_groups=mesh['line'=32,'scan'=16] {'line'}, dimensions={0} | all-to-all | bytes 262144 | tf_op jit(solution)/shard_map/all_to_all | solution.py:198
  160.6 0.7 reshape_reshape.3
  (227 shorter events, 22.0 us)
Async XLA Ops:
  1.0 25.8 %copy-start.20 = (f32[4,128]{1,0:T(4,128)}, f32[4,128]{1,0:T(4,128)S(1)}, u32[]{:S(2)}) copy-start(f32[4,128]{1,0:T(4,128)S(1)} %sqrt_bitcast_fusion) | copy-start | bytes 6148
  1.1 4.8 %copy-start.17 = (pred[128,128]{1,0:T(8,128)(4,1)}, pred[128,128]{1,0:T(8,128)(4,1)S(1)}, u32[]{:S(2)}) copy-start(pred[128,128]{1,0:T(8,128)(4,1)S(1)} %get-tuple-element.89) | copy-start | bytes 49156
  22.2 2.4 %copy-start.2 = (bf16[1,128,512]{2,1,0:T(8,128)(2,1)S(1)}, bf16[1,128,512]{2,1,0:T(8,128)(2,1)}, u32[]{:S(2)}) copy-start(bf16[1,128,512]{2,1,0:T(8,128)(2,1)} %param.13) | copy-start | bytes 393220
  22.3 2.3 %copy-start.22 = (f32[1,128,4]{1,2,0:T(4,128)S(1)}, f32[1,128,4]{1,2,0:T(4,128)}, u32[]{:S(2)}) copy-start(f32[1,128,4]{1,2,0:T(4,128)} %param.15) | copy-start | bytes 6148
  25.7 6.4 %copy-start.1 = (bf16[1,128,512]{2,1,0:T(8,128)(2,1)S(1)}, bf16[1,128,512]{2,1,0:T(8,128)(2,1)}, u32[]{:S(2)}) copy-start(bf16[1,128,512]{2,1,0:T(8,128)(2,1)} %param.11) | copy-start | bytes 393220
  25.7 7.1 %copy-start.7 = (bf16[32,1,4,512]{3,2,1,0:T(4,128)(2,1)S(1)}, bf16[32,1,4,512]{3,2,1,0:T(4,128)(2,1)}, u32[]{:S(2)}) copy-start(bf16[32,1,4,512]{3,2,1,0:T(4,128)(2,1)} %param.18) | copy-start | bytes 393220
  26.6 6.5 %copy-start.25 = (f32[32,1,4,4]{0,3,2,1:T(4,128)S(1)}, f32[32,1,4,4]{0,3,2,1:T(4,128)}, u32[]{:S(2)}) copy-start(f32[32,1,4,4]{0,3,2,1:T(4,128)} %param.19) | copy-start | bytes 6148
  26.6 6.7 %copy-start.19 = (f32[32,1,4,4]{0,3,2,1:T(4,128)S(1)}, f32[32,1,4,4]{0,3,2,1:T(4,128)}, u32[]{:S(2)}) copy-start(f32[32,1,4,4]{0,3,2,1:T(4,128)} %param.20) | copy-start | bytes 6148
  28.4 18.0 %collective-permute-start = (f32[4,128,256]{2,1,0:T(8,128)}, f32[4,128,256]{2,1,0:T(8,128)}, u32[]{:S(2)}, u32[]{:S(2)}) collective-permute-start(f32[4,128,256]{2,1,0:T(8,128)} %pad_maximum_fusion), channel_id=1, source_target_pairs={{0,1},{1,2},{2,3},{3,4},{4,5},{5,6},{6,7},{7,8},{8,9},{9,10},{10,1... | collective-permute-start | bytes 1572872 | tf_op jit(solution)/shard_map/ppermute | solution.py:13
  48.6 17.1 %collective-permute-start.1 = (f32[4,128,256]{1,2,0:T(8,128)S(1)}, f32[4,128,256]{1,2,0:T(8,128)S(1)}, u32[]{:S(2)}, u32[]{:S(2)}) collective-permute-start(f32[4,128,256]{1,2,0:T(8,128)S(1)} %pad_maximum_fusion.1), channel_id=1, source_target_pairs={{0,2},{1,3},{2,4},{3,5},{4,6},{5,7},{6,8},{7,9},{8,10},{9,11},{10,... | collective-permute-start | bytes 1572872 | tf_op jit(solution)/shard_map/ppermute | solution.py:13
  52.6 15.8 %copy-start.13 = (bf16[1,128,128]{2,1,0:T(8,128)(2,1)S(1)}, bf16[1,128,128]{2,1,0:T(8,128)(2,1)}, u32[]{:S(2)}) copy-start(bf16[1,128,128]{2,1,0:T(8,128)(2,1)} %get-tuple-element.73) | copy-start | bytes 98308
  52.6 15.8 %copy-start.14 = (bf16[1,128,128]{2,1,0:T(8,128)(2,1)S(1)}, bf16[1,128,128]{2,1,0:T(8,128)(2,1)}, u32[]{:S(2)}) copy-start(bf16[1,128,128]{2,1,0:T(8,128)(2,1)} %get-tuple-element.74) | copy-start | bytes 98308
  52.6 15.8 %copy-start.15 = (bf16[1,128,128]{2,1,0:T(8,128)(2,1)S(1)}, bf16[1,128,128]{2,1,0:T(8,128)(2,1)}, u32[]{:S(2)}) copy-start(bf16[1,128,128]{2,1,0:T(8,128)(2,1)} %get-tuple-element.75) | copy-start | bytes 98308
  52.6 15.8 %copy-start.16 = (bf16[1,128,128]{2,1,0:T(8,128)(2,1)S(1)}, bf16[1,128,128]{2,1,0:T(8,128)(2,1)}, u32[]{:S(2)}) copy-start(bf16[1,128,128]{2,1,0:T(8,128)(2,1)} %get-tuple-element.76) | copy-start | bytes 98308
  66.2 2.9 %copy-start.18 = (pred[128,128]{1,0:T(8,128)(4,1)S(1)}, pred[128,128]{1,0:T(8,128)(4,1)}, u32[]{:S(2)}) copy-start(pred[128,128]{1,0:T(8,128)(4,1)} %copy-done.17) | copy-start | bytes 49156
  66.2 2.9 %copy-start.21 = (f32[4,128]{1,0:T(4,128)S(1)}, f32[4,128]{1,0:T(4,128)}, u32[]{:S(2)}) copy-start(f32[4,128]{1,0:T(4,128)} %copy-done.20) | copy-start | bytes 6148
  67.1 14.1 %collective-permute-start.2 = (f32[4,128,256]{1,2,0:T(8,128)}, f32[4,128,256]{1,2,0:T(8,128)}, u32[]{:S(2)}, u32[]{:S(2)}) collective-permute-start(f32[4,128,256]{1,2,0:T(8,128)} %pad_maximum_fusion.2), channel_id=1, source_target_pairs={{0,4},{1,5},{2,6},{3,7},{4,8},{5,9},{6,10},{7,11},{8,12},{9,13},{1... | collective-permute-start | bytes 1572872 | tf_op jit(solution)/shard_map/ppermute | solution.py:13
  82.9 12.8 %copy-start.5 = (f32[1,128,128]{2,1,0:T(8,128)S(1)}, f32[1,128,128]{2,1,0:T(8,128)}, u32[]{:S(2)}) copy-start(f32[1,128,128]{2,1,0:T(8,128)} %get-tuple-element.63) | copy-start | bytes 196612
  82.9 12.8 %copy-start.6 = (f32[1,128,128]{2,1,0:T(8,128)S(1)}, f32[1,128,128]{2,1,0:T(8,128)}, u32[]{:S(2)}) copy-start(f32[1,128,128]{2,1,0:T(8,128)} %get-tuple-element.64) | copy-start | bytes 196612
  83.1 9.8 %collective-permute-start.3 = (f32[4,128,128]{1,2,0:T(8,128)S(1)}, f32[4,128,128]{1,2,0:T(8,128)S(1)}, u32[]{:S(2)}, u32[]{:S(2)}) collective-permute-start(f32[4,128,128]{1,2,0:T(8,128)S(1)} %add.162), channel_id=1, source_target_pairs={{0,8},{1,9},{2,10},{3,11},{4,12},{5,13},{6,14},{7,15},{16,24},{17,... | collective-permute-start | bytes 786440 | tf_op jit(solution)/shard_map/ppermute | solution.py:13
  84.7 20.2 %copy-start.30 = (f32[128]{0:T(128)S(1)}, f32[128]{0:T(128)}, u32[]{:S(2)}) copy-start(f32[128]{0:T(128)} %param.16) | copy-start | bytes 1540
  93.5 28.0 %copy-start.9 = (bf16[4,32,128]{2,1,0:T(8,128)(2,1)S(1)}, bf16[4,32,128]{2,1,0:T(8,128)(2,1)}, u32[]{:S(2)}) copy-start(bf16[4,32,128]{2,1,0:T(8,128)(2,1)} %get-tuple-element.77) | copy-start | bytes 98308
  93.5 28.0 %copy-start.10 = (bf16[4,32,128]{2,1,0:T(8,128)(2,1)S(1)}, bf16[4,32,128]{2,1,0:T(8,128)(2,1)}, u32[]{:S(2)}) copy-start(bf16[4,32,128]{2,1,0:T(8,128)(2,1)} %get-tuple-element.78) | copy-start | bytes 98308
  93.6 28.0 %copy-start.11 = (bf16[4,32,128]{2,1,0:T(8,128)(2,1)S(1)}, bf16[4,32,128]{2,1,0:T(8,128)(2,1)}, u32[]{:S(2)}) copy-start(bf16[4,32,128]{2,1,0:T(8,128)(2,1)} %get-tuple-element.79) | copy-start | bytes 98308
  93.6 28.0 %copy-start.12 = (bf16[4,32,128]{2,1,0:T(8,128)(2,1)S(1)}, bf16[4,32,128]{2,1,0:T(8,128)(2,1)}, u32[]{:S(2)}) copy-start(bf16[4,32,128]{2,1,0:T(8,128)(2,1)} %get-tuple-element.80) | copy-start | bytes 98308
  93.6 28.0 %copy-start.4 = (f32[4,128,128]{2,1,0:T(8,128)S(1)}, f32[4,128,128]{2,1,0:T(8,128)}, u32[]{:S(2)}) copy-start(f32[4,128,128]{2,1,0:T(8,128)} %copy-done.3) | copy-start | bytes 786436
  93.6 28.0 %copy-start.24 = (f32[16,32]{1,0:T(8,128)S(1)}, f32[16,32]{1,0:T(8,128)}, u32[]{:S(2)}) copy-start(f32[16,32]{1,0:T(8,128)} %copy-done.23) | copy-start | bytes 6148
  93.6 28.0 %copy-start.27 = (f32[16,32]{1,0:T(8,128)S(1)}, f32[16,32]{1,0:T(8,128)}, u32[]{:S(2)}) copy-start(f32[16,32]{1,0:T(8,128)} %copy-done.26) | copy-start | bytes 6148
  93.6 28.0 %copy-start.29 = (pred[32,32]{1,0:T(8,128)(4,1)S(1)}, pred[32,32]{1,0:T(8,128)(4,1)}, u32[]{:S(2)}) copy-start(pred[32,32]{1,0:T(8,128)(4,1)} %copy-done.28) | copy-start | bytes 3076
  93.6 10.5 %collective-permute-start.4 = (f32[4,128,128]{1,2,0:T(8,128)S(1)}, f32[4,128,128]{1,2,0:T(8,128)S(1)}, u32[]{:S(2)}, u32[]{:S(2)}) collective-permute-start(f32[4,128,128]{1,2,0:T(8,128)S(1)} %convolution_add_fusion.7), channel_id=1, source_target_pairs={{0,1},{1,2},{2,3},{3,4},{4,5},{5,6},{6,7},{7,8},{8,9},{9,10},{10,1... | collective-permute-start | bytes 786440 | tf_op jit(solution)/shard_map/ppermute | solution.py:13
  105.8 32.8 %all-to-all-start = ((bf16[1,32,4,512]{3,2,0,1:T(4,128)(2,1)}), bf16[1,32,4,512]{3,2,0,1:T(4,128)(2,1)S(1)}, u32[]{:S(2)}, u32[]{:S(2)}) async-start(bf16[1,32,4,512]{3,2,0,1:T(4,128)(2,1)} %bitcast.66), calls=%async_computation | async-start | bytes 262144 | tf_op jit(solution)/shard_map/all_to_all | solution.py:184
  121.6 17.6 %copy-start.31 = (f32[128]{0:T(128)S(1)}, f32[128]{0:T(128)}, u32[]{:S(2)}) copy-start(f32[128]{0:T(128)} %param.21) | copy-start | bytes 1540
  (6 other events, 9.3 us)
